TPU v7x, 32 devices: a whole 2x2x4 slice. The times are simulated.
32 devices in a mesh: dp: 8 (over z, x), spatial: 4 (over y, core).
Axes of the slice: x: 2, y: 2, z: 4, core: 2. Of those that a mesh axis runs over, the one named last changes fastest.
Arguments:
- fields: bfloat16 [8, 64, 128, 768], P('dp', 'spatial'), may hold values from -6 to 6
- norm_gain: float32 [768], replicated, may hold values from 0.5 to 1.5
- norm_shift: float32 [768], replicated, may hold values from -3 to 3
- first_weight: bfloat16 [2, 8, 96, 96], replicated, may hold values from -0.4375 to 0.4375
- first_bias: float32 [8, 192], replicated, may hold values from -3 to 3
- second_weight: bfloat16 [2, 8, 96, 96], replicated, may hold values from -0.4375 to 0.4375
- second_bias: float32 [8, 192], replicated, may hold values from -3 to 3
- cotangent: bfloat16 [8, 64, 128, 768], P('dp', 'spatial'), may hold values from -6 to 6
Outputs:
- block_output: bfloat16 [8, 64, 128, 768], P('dp', 'spatial')
- grad_fields: bfloat16 [8, 64, 128, 768], P('dp', 'spatial')
- grad_first: float32 [2, 8, 96, 96], replicated
- grad_first_bias: float32 [8, 192], replicated
- grad_second: float32 [2, 8, 96, 96], replicated
- grad_second_bias: float32 [8, 192], replicated
- grad_gain: float32 [768], replicated
- grad_shift: float32 [768], replicated
All inputs are finite; a program needn't handle non-finite values.
Results may differ from a plain program's by a relative error of at most 0.017.
The roundings to bfloat16 on the way count: a program that leaves them out, or rounds other values in their place, can miss the bound.
Values may be sent and summed in bfloat16 or wider, within the bound.
No kernel may reach another device: no remote copies, remote signals or barrier semaphores. Data moves between devices by JAX's collectives and lax.ppermute only.
A program may use at most 192 MiB of HBM per device.

v0:
```python
import math
import jax
import jax.numpy as jnp
from jax import lax
from jax.sharding import PartitionSpec as P

LAT = 64
LON = 128
BLOCKS = 8
BLOCK = 96
shrink_cut = 0.01
norm_epsilon = 1e-06
gelu_factor = 0.7978845608
gelu_cubic = 0.044715


def product(pattern, left_side, right_side):
    return jnp.einsum(pattern, left_side, right_side, preferred_element_type=jnp.float32)


def tables(count, mode_count, doubled):
    positions = jnp.arange(count, dtype=jnp.int32)
    orders = jnp.arange(mode_count, dtype=jnp.int32)
    phases = orders[:, None] * positions[None, :] % count
    angles = 2.0 * math.pi / count * phases.astype(jnp.float32)
    factor = jnp.ones((mode_count, 1), jnp.float32) / math.sqrt(count)
    if doubled:
        factor = factor * jnp.where(orders == 0, 1.0, 2.0).astype(jnp.float32)[:, None]
    return (
        (jnp.cos(angles) * factor).astype(jnp.bfloat16),
        (jnp.sin(angles) * factor).astype(jnp.bfloat16),
    )


def rotate(values):
    half_width = values.shape[-1] // 2
    return jnp.concatenate([values[..., half_width:], -values[..., :half_width]], axis=-1)


def along_lon(real_part, cos_table, sin_table):
    real_sum = product("bhwnp,mw->bhmnp", real_part, cos_table)
    imag_sum = -product("bhwnp,mw->bhmnp", real_part, sin_table)
    return jnp.concatenate([real_sum, imag_sum], axis=-1).astype(jnp.bfloat16)


def back_lon(spectral, cos_table, sin_table):
    half_width = spectral.shape[-1] // 2
    return product("bhmnp,mw->bhwnp", spectral[..., :half_width], cos_table) - product(
        "bhmnp,mw->bhwnp", spectral[..., half_width:], sin_table
    )


def along_lat(spectral, cos_table, sin_table):
    direct = product("kh,bhmnp->bkmnp", cos_table, spectral)
    turned = product("kh,bhmnp->bkmnp", sin_table, spectral)
    return (direct + rotate(turned)).astype(jnp.bfloat16)


def back_lat(spectral, cos_table, sin_table):
    direct = product("kh,bhmnp->bkmnp", cos_table, spectral)
    turned = product("kh,bhmnp->bkmnp", sin_table, spectral)
    return (direct - rotate(turned)).astype(jnp.bfloat16)


def real_blocks(weight):
    upper_rows = jnp.concatenate([weight[0], weight[1]], axis=-1)
    bottom = jnp.concatenate([-weight[1], weight[0]], axis=-1)
    return jnp.concatenate([upper_rows, bottom], axis=1)


def fold_blocks(gradient):
    half_width = gradient.shape[-1] // 2
    real_grad = gradient[:, :half_width, :half_width] + gradient[:, half_width:, half_width:]
    imag_grad = gradient[:, :half_width, half_width:] - gradient[:, half_width:, :half_width]
    return jnp.stack([real_grad, imag_grad])


def gelu_value(values):
    inner = jnp.tanh(gelu_factor * (values + gelu_cubic * values * values * values))
    return 0.5 * values * (1.0 + inner)


def gelu_slope(values):
    inner = jnp.tanh(gelu_factor * (values + gelu_cubic * values * values * values))
    return 0.5 * (1.0 + inner) + 0.5 * values * (1.0 - inner * inner) * gelu_factor * (
        1.0 + 3.0 * gelu_cubic * values * values
    )


def spectral_forward(transformed, first_real, first_bias, second_real, second_bias):
    hidden_pre = product("bkmnp,npq->bkmnq", transformed, first_real) + first_bias
    hidden = gelu_value(hidden_pre).astype(jnp.bfloat16)
    output_pre = product("bkmnp,npq->bkmnq", hidden, second_real) + second_bias
    shrunk = (output_pre - shrink_cut * jnp.tanh(output_pre / shrink_cut)).astype(jnp.bfloat16)
    return (hidden_pre, hidden, output_pre, shrunk)


def spectral_backward(
    transformed, hidden_pre, hidden, output_pre, grad_shrunk, first_real, second_real
):
    bend = jnp.tanh(output_pre / shrink_cut)
    grad_outpre = (grad_shrunk.astype(jnp.float32) * bend * bend).astype(jnp.bfloat16)
    grad_second = product("bkmnp,bkmnq->npq", hidden, grad_outpre)
    grad_second_bias = jnp.sum(grad_outpre.astype(jnp.float32), axis=(0, 1, 2))
    grad_hidden = product("bkmnq,npq->bkmnp", grad_outpre, second_real)
    grad_hidpre = (grad_hidden * gelu_slope(hidden_pre)).astype(jnp.bfloat16)
    grad_first = product("bkmnp,bkmnq->npq", transformed, grad_hidpre)
    grad_first_bias = jnp.sum(grad_hidpre.astype(jnp.float32), axis=(0, 1, 2))
    grad_transformed = product("bkmnq,npq->bkmnp", grad_hidpre, first_real).astype(jnp.bfloat16)
    return (grad_transformed, grad_first, grad_first_bias, grad_second, grad_second_bias)


def normalize(fields):
    values = fields.astype(jnp.float32)
    center = jnp.mean(values, axis=-1, keepdims=True)
    spread = jnp.mean((values - center) ** 2, axis=-1, keepdims=True)
    inverse_std = lax.rsqrt(spread + norm_epsilon)
    return ((values - center) * inverse_std, inverse_std)


def norm_backward(grad_scaled, normed, inverse_std, norm_gain):
    grad_normed = grad_scaled * norm_gain
    mean_grad = jnp.mean(grad_normed, axis=-1, keepdims=True)
    mean_cross = jnp.mean(grad_normed * normed, axis=-1, keepdims=True)
    return inverse_std * (grad_normed - mean_grad - normed * mean_cross)


def local(
    fields, norm_gain, norm_shift, first_weight, first_bias, second_weight, second_bias, cotangent
):
    samples, band_rows, longitudes, channels = fields.shape
    mode_count = longitudes // 2
    ahead_cos, ahead_sin = tables(longitudes, mode_count, False)
    back_cos, back_sin = tables(longitudes, mode_count, True)
    polar_cos, polar_sin = tables(LAT, LAT, False)
    first_real = real_blocks(first_weight)
    second_real = real_blocks(second_weight)
    block_shape = (samples, band_rows, longitudes, BLOCKS, BLOCK)
    normed, inverse_std = normalize(fields)
    scaled = (normed * norm_gain + norm_shift).astype(jnp.bfloat16)
    spectral = along_lon(scaled.reshape(block_shape), ahead_cos, ahead_sin)
    grad_returned = along_lon(cotangent.reshape(block_shape), back_cos, back_sin)
    columns = lax.all_to_all(spectral, "spatial", split_axis=2, concat_axis=1, tiled=True)
    transformed = along_lat(columns, polar_cos, polar_sin)
    hidden_pre, hidden, output_pre, shrunk = spectral_forward(
        transformed, first_real, first_bias, second_real, second_bias
    )
    returned = back_lat(shrunk, polar_cos, polar_sin)
    banded = lax.all_to_all(returned, "spatial", split_axis=1, concat_axis=2, tiled=True)
    mixed = back_lon(banded, back_cos, back_sin).reshape(fields.shape)
    block_output = (fields.astype(jnp.float32) + scaled.astype(jnp.float32) + mixed).astype(
        jnp.bfloat16
    )
    grad_columns = lax.all_to_all(grad_returned, "spatial", split_axis=2, concat_axis=1, tiled=True)
    grad_shrunk = along_lat(grad_columns, polar_cos, polar_sin)
    grad_transformed, g_first, g_first_bias, g_second, g_second_bias = spectral_backward(
        transformed, hidden_pre, hidden, output_pre, grad_shrunk, first_real, second_real
    )
    grad_spectral = back_lat(grad_transformed, polar_cos, polar_sin)
    grad_banded = lax.all_to_all(grad_spectral, "spatial", split_axis=1, concat_axis=2, tiled=True)
    grad_scaled = cotangent.astype(jnp.float32) + back_lon(
        grad_banded, ahead_cos, ahead_sin
    ).reshape(fields.shape)
    grad_fields = (
        cotangent.astype(jnp.float32) + norm_backward(grad_scaled, normed, inverse_std, norm_gain)
    ).astype(jnp.bfloat16)
    g_gain = jnp.sum(grad_scaled * normed, axis=(0, 1, 2))
    g_shift = jnp.sum(grad_scaled, axis=(0, 1, 2))
    terms = (
        fold_blocks(g_first),
        g_first_bias,
        fold_blocks(g_second),
        g_second_bias,
        g_gain,
        g_shift,
    )
    summed = lax.psum(
        (terms[0], terms[1], terms[2], terms[3], terms[4], terms[5]), ("dp", "spatial")
    )
    token_total = lax.axis_size("dp") * samples * LAT * LON
    scale = 1.0 / math.sqrt(token_total)
    return (
        block_output,
        grad_fields,
        summed[0] * scale,
        summed[1] * scale,
        summed[2] * scale,
        summed[3] * scale,
        summed[4] * scale,
        summed[5] * scale,
    )


def solution(mesh):
    return jax.shard_map(
        local,
        mesh=mesh,
        in_specs=(
            P("dp", "spatial", None, None),
            P(),
            P(),
            P(),
            P(),
            P(),
            P(),
            P("dp", "spatial", None, None),
        ),
        out_specs=(
            P("dp", "spatial", None, None),
            P("dp", "spatial", None, None),
            P(),
            P(),
            P(),
            P(),
            P(),
            P(),
        ),
        check_vma=False,
    )
```

profile of v0, /device:TPU:0, one launch (start us, length us, event | category | flops | bytes accessed | tf_op | source)
XLA Modules:
  0.0 488.9 jit_solution(11215165672078418992)
XLA Ops:
  17.3 4.4 copy.61
  21.7 5.1 %all-to-all-start.2 = ((bf16[1,16,64,8,192]{4,3,1,0,2:T(8,128)(2,1)}), bf16[1,16,64,8,192]{4,3,1,0,2:T(8,128)(2,1)}, u32[]{:S(2)}, u32[]{:S(2)}) async-start(bf16[1,16,64,8,192]{4,3,1,0,2:T(8,128)(2,1)} %copy.61), calls=%async_computation.2 | async-start | bytes 8388608 | tf_op jit(solution)/shard_map/all_to_all | solution.py:154
  39.8 4.5 copy.52
  44.2 31.5 %all-to-all-done.2 = bf16[1,16,64,8,192]{4,3,1,0,2:T(8,128)(2,1)} async-done(((bf16[1,16,64,8,192]{4,3,1,0,2:T(8,128)(2,1)}), bf16[1,16,64,8,192]{4,3,1,0,2:T(8,128)(2,1)}, u32[]{:S(2)}, u32[]{:S(2)}) %all-to-all-start.2) | async-done | bytes 3145760 | tf_op jit(solution)/shard_map/all_to_all | solution.py:154
  75.8 5.4 %all-to-all-start = ((bf16[1,16,64,8,192]{4,3,1,0,2:T(8,128)(2,1)}), bf16[1,16,64,8,192]{4,3,1,0,2:T(8,128)(2,1)}, u32[]{:S(2)}, u32[]{:S(2)}) async-start(bf16[1,16,64,8,192]{4,3,1,0,2:T(8,128)(2,1)} %copy.52), calls=%async_computation | async-start | bytes 8388608 | tf_op jit(solution)/shard_map/all_to_all | solution.py:143
  87.3 5.5 %copy.62 = bf16[1,16,4,16,8,192]{5,1,2,4,3,0:T(8,128)(2,1)} copy(bf16[1,16,4,16,8,192]{5,4,1,3,2,0:T(8,128)(2,1)} %bitcast.62) | data formatting | bytes 6291456 | tf_op jit(solution)/shard_map/all_to_all | solution.py:154
  92.7 36.6 %all-to-all-done = bf16[1,16,64,8,192]{4,3,1,0,2:T(8,128)(2,1)} async-done(((bf16[1,16,64,8,192]{4,3,1,0,2:T(8,128)(2,1)}), bf16[1,16,64,8,192]{4,3,1,0,2:T(8,128)(2,1)}, u32[]{:S(2)}, u32[]{:S(2)}) %all-to-all-start) | async-done | bytes 3145760 | tf_op jit(solution)/shard_map/all_to_all | solution.py:143
  132.8 4.6 convolution_bitcast_fusion
  137.4 9.3 %fusion.218 = (f32[1,64,16,8,96]{4,1,3,2,0:T(8,128)}, f32[1,64,16,8,96]{4,1,3,2,0:T(8,128)}) fusion(f32[1,64,16,8,192]{4,1,3,2,0:T(8,128)} %convolution_bitcast_fusion), kind=kLoop, calls=%fused_computation.264 | loop fusion | flops 786432 | bytes 12582912 | tf_op jit(solution)/shard_map/slice | solution.py:37
  146.7 4.9 fusion.31
  156.9 3.7 fusion.37
  166.2 4.9 fusion.217
  171.0 7.6 %fusion.9 = bf16[1,64,16,8,192]{4,1,3,2,0:T(8,128)(2,1)S(1)} fusion(f32[1,64,16,8,96]{4,1,3,2,0:T(8,128)} %get-tuple-element.39, f32[1,64,16,8,96]{4,1,3,2,0:T(8,128)} %get-tuple-element.38, f32[8,192,64,16]{1,2,3,0:T(8,128)} %copy-done.3, f32[8,192]{1,0:T(8,128)S(1)} %copy-done.21), kind=kOutput, calls=%fused_computation.17 | convolution fusion | flops 213975040 | bytes 15734784 | tf_op jit(solution)/shard_map/kh,bhmnp->bkmnp/dot_general | solution.py:18
  178.7 4.4 copy.57
  183.1 4.9 all-to-all-start.1
  187.9 6.8 %fusion.61 = f32[1,64,16,8,192]{4,1,2,3,0:T(8,128)} fusion(bf16[64,16,8,192]{3,0,2,1:T(8,128)(2,1)} %bitcast.315), kind=kOutput, calls=%fused_computation.87 | convolution fusion | flops 201392128 | bytes 9437184 | tf_op jit(solution)/shard_map/kh,bhmnp->bkmnp/dot_general | solution.py:18
  194.8 8.6 %fusion.216 = (f32[1,64,16,8,96]{4,1,2,3,0:T(8,128)S(1)}, f32[1,64,16,8,96]{4,1,2,3,0:T(8,128)}) fusion(f32[1,64,16,8,192]{4,1,2,3,0:T(8,128)} %fusion.61), kind=kLoop, calls=%fused_computation.262 | loop fusion | flops 786432 | bytes 12582912 | tf_op jit(solution)/shard_map/slice | solution.py:37
  203.4 7.0 %convert_reduce_fusion.1 = (f32[8,192]{1,0:T(8,128)}, bf16[1,64,16,8,192]{4,1,2,3,0:T(8,128)(2,1)S(1)}) fusion(f32[8,192]{1,0:T(8,128)S(1)} %copy-done.22, f32[8,192,64,16]{1,2,3,0:T(8,128)} %copy-done.3, f32[1,64,16,8,96]{4,1,2,3,0:T(8,128)} %get-tuple-element.37, f32[1,64,16,8,96]{4,1,2,3,0:T(8,128)S(1)} %get-tuple-element.36, ...), kind=kOutput, calls=%fused_computation.29 | convolution fusion | flops 218692096 | bytes 18886656 | tf_op jit(solution)/shard_map/kh,bhmnp->bkmnp/dot_general | solution.py:18
  210.4 11.2 %convert_reduce_fusion.2 = (f32[8,192]{1,0:T(8,128)}, bf16[1,64,16,8,192]{4,1,2,3,0:T(8,128)(2,1)S(1)}) fusion(f32[8,192]{1,0:T(8,128)S(1)} %copy-done.30, f32[8,192,64,16]{1,2,3,0:T(8,128)} %copy-done.7, bf16[1,64,16,8,192]{4,1,2,3,0:T(8,128)(2,1)S(1)} %get-tuple-element.55, bf16[8,96,96]{2,1,0:T(8,128)(2,1)S(1)} %copy-done.18, ...), kind=kOutput, calls=%fused_computation.30 | convolution fusion | flops 640940544 | bytes 13037568 | tf_op jit(solution)/shard_map/bkmnq,npq->bkmnp/dot_general | solution.py:18
  223.7 4.6 fusion.58
  228.3 9.2 %fusion.215 = (f32[1,64,16,8,96]{4,1,3,2,0:T(8,128)}, f32[1,64,16,8,96]{4,1,3,2,0:T(8,128)}) fusion(f32[1,64,16,8,192]{4,1,3,2,0:T(8,128)} %fusion.58), kind=kLoop, calls=%fused_computation.261 | loop fusion | flops 786432 | bytes 12582912 | tf_op jit(solution)/shard_map/slice | solution.py:37
  237.5 4.8 fusion.11
  242.4 4.4 copy.67
  246.8 3.7 fusion.76
  251.5 4.4 fusion.79
  255.9 4.8 all-to-all-start.3
  266.0 136.6 %all-reduce.4.cloned.1.call-done = (f32[2,8,96,96]{3,2,1,0:T(8,128)}, f32[2,8,96,96]{3,2,1,0:T(8,128)}) async-done(((f32[2,8,96,96]{3,2,1,0:T(8,128)}, f32[2,8,96,96]{3,2,1,0:T(8,128)}), (f32[2,8,96,96]{3,2,1,0:T(8,128)}, f32[2,8,96,96]{3,2,1,0:T(8,128)})) %all-reduce.4.cloned.1.call-update) | async-done | bytes 1179664 | tf_op jit(solution)/shard_map/psum | solution.py:177
  410.1 5.7 %convolution_subtract_fusion.1 = f32[128,16,8,96]{0,3,2,1:T(8,128)} fusion(f32[128,16,8,96]{0,3,2,1:T(8,128)S(1)} %fusion.73, bf16[1,16,64,8,192]{4,2,3,1,0:T(8,128)(2,1)S(1)} %bitcast.326, f32[64]{0:T(128)S(1)} %copy-done.28), kind=kOutput, calls=%fused_computation.90 | convolution fusion | flops 203030528 | bytes 14680576 | tf_op jit(solution)/shard_map/bhmnp,mw->bhwnp/dot_general | solution.py:18
  423.2 4.4 fusion.25
  427.6 6.1 %fusion.27 = (bf16[1,16,128,768]{2,3,1,0:T(8,128)(2,1)}, bf16[1,16,128,768]{2,3,1,0:T(8,128)(2,1)}) fusion(bf16[1,16,128,768]{2,3,1,0:T(8,128)(2,1)S(1)} %copy.51, bf16[1,16,128,768]{2,3,1,0:T(8,128)(2,1)S(1)} %copy-done.1, f32[16,128]{1,0:T(8,128)S(1)} %get-tuple-element.56, f32[16,128]{1,0:T(8,128)S(1)} %get-tuple-element.57, f32[768]{0:T(1024)S(1)} %copy-done.20, ...), kind=kLoop, calls=%fused_computation.47 | loop fusion | flops 29884416 | bytes 25204736 | tf_op jit(solution)/shard_map/convert_element_type | solution.py:166
  433.7 4.8 copy.71
  441.3 39.4 %all-reduce = (f32[8,192]{1,0:T(8,128)S(1)}, f32[8,192]{1,0:T(8,128)S(1)}, f32[768]{0:T(1024)S(1)}, f32[768]{0:T(1024)S(1)}) all-reduce(f32[8,192]{1,0:T(8,128)S(1)} %copy-done.26, f32[8,192]{1,0:T(8,128)S(1)} %copy-done.23, f32[768]{0:T(1024)S(1)} %get-tuple-element.24, ...), channel_id=1, replica_groups=mesh['dp'=8,'spatial'=4] {'dp','spatial'}, use_global_device_ids=true, to_apply=%region_6.7 | all-reduce | flops 4608 | bytes 36864 | tf_op jit(solution)/shard_map/psum | solution.py:177
  (112 shorter events, 70.3 us)
Async XLA Ops:
  7.2 5.9 %copy-start.27 = (f32[64]{0:T(128)}, f32[64]{0:T(128)S(1)}, u32[]{:S(2)}) copy-start(f32[64]{0:T(128)S(1)} %fusion.123) | copy-start | bytes 772
  10.7 4.8 copy-start
  21.7 54.1 %all-to-all-start.2 = ((bf16[1,16,64,8,192]{4,3,1,0,2:T(8,128)(2,1)}), bf16[1,16,64,8,192]{4,3,1,0,2:T(8,128)(2,1)}, u32[]{:S(2)}, u32[]{:S(2)}) async-start(bf16[1,16,64,8,192]{4,3,1,0,2:T(8,128)(2,1)} %copy.61), calls=%async_computation.2 | async-start | bytes 8388608 | tf_op jit(solution)/shard_map/all_to_all | solution.py:154
  75.8 53.6 %all-to-all-start = ((bf16[1,16,64,8,192]{4,3,1,0,2:T(8,128)(2,1)}), bf16[1,16,64,8,192]{4,3,1,0,2:T(8,128)(2,1)}, u32[]{:S(2)}, u32[]{:S(2)}) async-start(bf16[1,16,64,8,192]{4,3,1,0,2:T(8,128)(2,1)} %copy.52), calls=%async_computation | async-start | bytes 8388608 | tf_op jit(solution)/shard_map/all_to_all | solution.py:143
  146.7 4.9 %copy-start.11 = (bf16[8,96,96]{2,1,0:T(8,128)(2,1)S(1)}, bf16[8,96,96]{2,1,0:T(8,128)(2,1)}, u32[]{:S(2)}) copy-start(bf16[8,96,96]{2,1,0:T(8,128)(2,1)} %get-tuple-element.51) | copy-start | bytes 442372
  151.6 5.2 %copy-start.13 = (bf16[8,96,96]{2,1,0:T(8,128)(2,1)S(1)}, bf16[8,96,96]{2,1,0:T(8,128)(2,1)}, u32[]{:S(2)}) copy-start(bf16[8,96,96]{2,1,0:T(8,128)(2,1)} %fusion.213) | copy-start | bytes 442372
  151.6 5.2 %copy-start.15 = (bf16[8,96,96]{2,1,0:T(8,128)(2,1)S(1)}, bf16[8,96,96]{2,1,0:T(8,128)(2,1)}, u32[]{:S(2)}) copy-start(bf16[8,96,96]{2,1,0:T(8,128)(2,1)} %get-tuple-element.48) | copy-start | bytes 442372
  151.6 5.2 %copy-start.17 = (bf16[8,96,96]{2,1,0:T(8,128)(2,1)S(1)}, bf16[8,96,96]{2,1,0:T(8,128)(2,1)}, u32[]{:S(2)}) copy-start(bf16[8,96,96]{2,1,0:T(8,128)(2,1)} %get-tuple-element.49) | copy-start | bytes 442372
  151.6 5.2 %copy-start.29 = (f32[8,192]{1,0:T(8,128)S(1)}, f32[8,192]{1,0:T(8,128)}, u32[]{:S(2)}) copy-start(f32[8,192]{1,0:T(8,128)} %param.12) | copy-start | bytes 18436
  153.6 3.3 copy-start.7
  156.9 7.0 %copy-start.21 = (f32[8,192]{1,0:T(8,128)S(1)}, f32[8,192]{1,0:T(8,128)}, u32[]{:S(2)}) copy-start(f32[8,192]{1,0:T(8,128)} %param.14) | copy-start | bytes 18436
  160.6 3.2 copy-start.3
  183.1 72.8 %all-to-all-start.1 = ((bf16[1,64,16,8,192]{4,3,2,0,1:T(8,128)(2,1)}), bf16[1,64,16,8,192]{4,3,2,0,1:T(8,128)(2,1)}, u32[]{:S(2)}, u32[]{:S(2)}) async-start(bf16[1,64,16,8,192]{4,3,2,0,1:T(8,128)(2,1)} %copy.57), calls=%async_computation.1 | async-start | bytes 8388608 | tf_op jit(solution)/shard_map/all_to_all | solution.py:149
  194.8 8.6 %copy-start.2 = (bf16[1,16,4,16,8,192]{5,1,2,4,3,0:T(8,128)(2,1)S(1)}, bf16[1,16,4,16,8,192]{5,1,2,4,3,0:T(8,128)(2,1)}, u32[]{:S(2)}) copy-start(bf16[1,16,4,16,8,192]{5,1,2,4,3,0:T(8,128)(2,1)} %copy.62) | copy-start | bytes 9437188
  194.8 8.6 %copy-start.22 = (f32[8,192]{1,0:T(8,128)S(1)}, f32[8,192]{1,0:T(8,128)}, u32[]{:S(2)}) copy-start(f32[8,192]{1,0:T(8,128)} %param.14) | copy-start | bytes 18436
  203.4 7.0 %copy-start.14 = (bf16[8,96,96]{2,1,0:T(8,128)(2,1)S(1)}, bf16[8,96,96]{2,1,0:T(8,128)(2,1)}, u32[]{:S(2)}) copy-start(bf16[8,96,96]{2,1,0:T(8,128)(2,1)} %fusion.213) | copy-start | bytes 442372
  203.4 7.0 %copy-start.16 = (bf16[8,96,96]{2,1,0:T(8,128)(2,1)S(1)}, bf16[8,96,96]{2,1,0:T(8,128)(2,1)}, u32[]{:S(2)}) copy-start(bf16[8,96,96]{2,1,0:T(8,128)(2,1)} %get-tuple-element.48) | copy-start | bytes 442372
  203.4 7.0 %copy-start.18 = (bf16[8,96,96]{2,1,0:T(8,128)(2,1)S(1)}, bf16[8,96,96]{2,1,0:T(8,128)(2,1)}, u32[]{:S(2)}) copy-start(bf16[8,96,96]{2,1,0:T(8,128)(2,1)} %get-tuple-element.49) | copy-start | bytes 442372
  203.4 7.0 %copy-start.30 = (f32[8,192]{1,0:T(8,128)S(1)}, f32[8,192]{1,0:T(8,128)}, u32[]{:S(2)}) copy-start(f32[8,192]{1,0:T(8,128)} %param.12) | copy-start | bytes 18436
  210.4 11.2 %copy-start.9 = (bf16[1,64,16,8,192]{4,1,2,3,0:T(8,128)(2,1)}, bf16[1,64,16,8,192]{4,1,2,3,0:T(8,128)(2,1)S(1)}, u32[]{:S(2)}) copy-start(bf16[1,64,16,8,192]{4,1,2,3,0:T(8,128)(2,1)S(1)} %get-tuple-element.55) | copy-start | bytes 9437188
  210.4 11.2 %copy-start.12 = (bf16[8,96,96]{2,1,0:T(8,128)(2,1)S(1)}, bf16[8,96,96]{2,1,0:T(8,128)(2,1)}, u32[]{:S(2)}) copy-start(bf16[8,96,96]{2,1,0:T(8,128)(2,1)} %get-tuple-element.51) | copy-start | bytes 442372
  242.4 4.4 copy-start.5
  242.4 9.2 %slice-start.2 = ((s8[8388608]{0:T(1024)(128)(4,1)}), s8[4194304]{0:T(1024)(128)(4,1)S(1)}, s32[]{:S(2)}) async-start(s8[8388608]{0:T(1024)(128)(4,1)} %bitcast.327), calls=%async_computation.7 | async-start | bytes 8388608
  246.8 4.7 slice-start.3
  246.8 4.7 copy-start.10
  255.9 159.8 %all-to-all-start.3 = ((bf16[1,64,16,8,192]{4,3,2,0,1:T(8,128)(2,1)}), bf16[1,64,16,8,192]{4,3,2,0,1:T(8,128)(2,1)}, u32[]{:S(2)}, u32[]{:S(2)}) async-start(bf16[1,64,16,8,192]{4,3,2,0,1:T(8,128)(2,1)} %copy.67), calls=%async_computation.3 | async-start | bytes 8388608 | tf_op jit(solution)/shard_map/all_to_all | solution.py:160
  260.7 141.9 %all-reduce.4.cloned.1.call-start = ((), (), s32[]{:S(2)}) async-start(), calls=%async_computation.4 | async-start | bytes 3145728 | tf_op jit(solution)/shard_map/psum | solution.py:177
  405.2 3.4 copy-start.28
  419.2 8.4 %slice-start = ((s8[6291456]{0:T(1024)(128)(4,1)}), s8[4194304]{0:T(1024)(128)(4,1)S(1)}, s32[]{:S(2)}) async-start(s8[6291456]{0:T(1024)(128)(4,1)} %bitcast.321), calls=%async_computation.5 | async-start | bytes 8388608
  420.6 7.0 %slice-start.1 = ((s8[6291456]{0:T(1024)(128)(4,1)}), s8[2097152]{0:T(1024)(128)(4,1)S(1)}, s32[]{:S(2)}) async-start(s8[6291456]{0:T(1024)(128)(4,1)} %bitcast.321), calls=%async_computation.6 | async-start | bytes 4194304
  423.2 4.4 copy-start.25
  433.7 4.8 copy-start.6
  (8 other events, 17.4 us)
Sparse Core Ops, SparseCore 0:
  267.6 134.9 all-reduce.3
where the time goes:
time: 495 us; the launch traced here: 489 us
  waiting for transfers between devices  205 us (41%)
  matrix products  89 us (18%)
  other arithmetic  61 us (12%)
  local copies, waits for them, and re-layouts  59.3 us (12%)
  blocking collectives  39.4 us (8%)
  starting transfers between devices  20.7 us (4%)
  between operations  14.8 us (3%)
    psum x1, waiting for transfers between devices, local(): lax.psum((terms[0], terms[1], terms[2], terms[3], terms[4], terms[5]), ('...  137 us
    dot_general x22, matrix products, product(): jnp.einsum(pattern, left_side, right_side, preferred_element_type=jnp.flo...  89 us
    psum x1, blocking collectives, local(): lax.psum((terms[0], terms[1], terms[2], terms[3], terms[4], terms[5]), ('...  39.4 us
    all_to_all x1, waiting for transfers between devices, local(): lax.all_to_all(spectral, 'spatial', split_axis=2, concat_axis=1, tiled=True)  36.6 us
    slice x4, other arithmetic, rotate(): values[..., half_width:]  32 us
    all_to_all x1, waiting for transfers between devices, local(): lax.all_to_all(grad_returned, 'spatial', split_axis=2, concat_axis=1, til...  31.5 us
    unnamed x74, local copies, waits for them, and re-layouts  22.4 us
  transfers between devices with their start and end apart: 5, of which 3 were waited for; matrix products, arithmetic and copies ran while one was open for 23% of the time, Pallas kernels for 0%

commit v1 on v0

--- a/solution.py
+++ b/solution.py
@@ -12,6 +12,28 @@
 norm_epsilon = 1e-06
 gelu_factor = 0.7978845608
 gelu_cubic = 0.044715
+
+
+def split_up(x, dim, peers):
+    before, after = (x.shape[:dim], x.shape[dim + 1 :])
+    return jnp.moveaxis(x.reshape(*before, peers, -1, *after), dim, 0)
+
+
+def joined_along(tiles, dim):
+    tiles = jnp.moveaxis(tiles, 0, dim)
+    shape = tiles.shape
+    return tiles.reshape(*shape[:dim], shape[dim] * shape[dim + 1], *shape[dim + 2 :])
+
+
+def exchange_in_pairs(shard, axis, split_dim, concat_dim):
+    size, index = (lax.axis_size(axis), lax.axis_index(axis))
+    blocks = split_up(shard, split_dim, size)
+    outs = [blocks[index]]
+    for step in range(1, size):
+        sent = blocks[index ^ step]
+        outs.append(lax.ppermute(sent, axis, [(i, i ^ step) for i in range(size)]))
+    blocks = jnp.stack(outs)[index ^ jnp.arange(size)]
+    return joined_along(blocks, concat_dim)
 
 
 def product(pattern, left_side, right_side):
@@ -151,7 +173,7 @@
     block_output = (fields.astype(jnp.float32) + scaled.astype(jnp.float32) + mixed).astype(
         jnp.bfloat16
     )
-    grad_columns = lax.all_to_all(grad_returned, "spatial", split_axis=2, concat_axis=1, tiled=True)
+    grad_columns = exchange_in_pairs(grad_returned, "spatial", 2, 1)
     grad_shrunk = along_lat(grad_columns, polar_cos, polar_sin)
     grad_transformed, g_first, g_first_bias, g_second, g_second_bias = spectral_backward(
         transformed, hidden_pre, hidden, output_pre, grad_shrunk, first_real, second_real

time: 495 us -> 476 us (0.962)
  waiting for transfers between devices: 205 us -> 172 us
  matrix products: 89 us -> 100 us
    all_to_all x1 -> x0, waiting for transfers between devices: 31.5 us -> none  [local(): lax.all_to_all(grad_returned, 'spatial', split_axis=2, concat_axis=1, til...]
    all_to_all x1, waiting for transfers between devices: 36.6 us -> 22.4 us  [local(): lax.all_to_all(spectral, 'spatial', split_axis=2, concat_axis=1, tiled=True)]
    ppermute x0 -> x3, waiting for transfers between devices: none -> 12.7 us  [exchange_in_pairs(): outs.append(lax.ppermute(sent, axis, [(i, i ^ step) for i in range(size)]))]
    dot_general x22, matrix products: 89 us -> 100 us  [product(): jnp.einsum(pattern, left_side, right_side, preferred_element_type=jnp.flo...]
    another operation x0 -> x4, local copies, waits for them, and re-layouts: none -> 5.84 us
    all_to_all x1 -> x0, local copies, waits for them, and re-layouts: 5.46 us -> none  [local(): lax.all_to_all(grad_returned, 'spatial', split_axis=2, concat_axis=1, til...]
    slice x4, other arithmetic: 32 us -> 26.7 us  [rotate(): values[..., half_width:]]
    all_to_all x1 -> x0, starting transfers between devices: 5.14 us -> none  [local(): lax.all_to_all(grad_returned, 'spatial', split_axis=2, concat_axis=1, til...]
  transfers between devices with their start and end apart: 5 -> 7, of which waited for: 3 -> 3; matrix products, arithmetic and copies ran while one was open for 23% -> 27% of each run, Pallas kernels for 0% -> 0%
where the time goes in v1:
time: 476 us; the launch traced here: 470 us
  waiting for transfers between devices  172 us (36%)
  matrix products  100 us (21%)
  other arithmetic  63.6 us (13%)
  local copies, waits for them, and re-layouts  60.9 us (13%)
  blocking collectives  39.4 us (8%)
  starting transfers between devices  18.5 us (4%)
  between operations  14.9 us (3%)
    psum x1, waiting for transfers between devices, local(): lax.psum((terms[0], terms[1], terms[2], terms[3], terms[4], terms[5]), ('...  137 us
    dot_general x22, matrix products, product(): jnp.einsum(pattern, left_side, right_side, preferred_element_type=jnp.flo...  100 us
    psum x1, blocking collectives, local(): lax.psum((terms[0], terms[1], terms[2], terms[3], terms[4], terms[5]), ('...  39.4 us
    slice x4, other arithmetic, rotate(): values[..., half_width:]  26.7 us
    unnamed x70, local copies, waits for them, and re-layouts  23 us
    all_to_all x1, waiting for transfers between devices, local(): lax.all_to_all(spectral, 'spatial', split_axis=2, concat_axis=1, tiled=True)  22.4 us
    ppermute x3, waiting for transfers between devices, exchange_in_pairs(): outs.append(lax.ppermute(sent, axis, [(i, i ^ step) for i in range(size)]))  12.7 us
  transfers between devices with their start and end apart: 7, of which 3 were waited for; matrix products, arithmetic and copies ran while one was open for 27% of the time, Pallas kernels for 0%

profile of v1, /device:TPU:0, one launch (start us, length us, event | category | flops | bytes accessed | tf_op | source)
XLA Modules:
  0.0 470.1 jit_solution(11660900534651097361)
XLA Ops:
  10.7 3.8 negate_convert_fusion
  18.2 5.0 %fusion.84 = (bf16[1,16,1,16,8,192]{5,3,2,4,1,0:T(8,128)(2,1)}, bf16[1,16,1,16,8,192]{5,3,2,4,1,0:T(8,128)(2,1)S(1)}, bf16[1,16,1,16,8,192]{5,3,2,4,1,0:T(8,128)(2,1)S(1)}, bf16[1,16,1,16,8,192]{5,3,2,4,1,0:T(8,128)(2,1)S(1)}) fusion(s32[]{:T(128)S(6)} %select_n.82, bf16[1,16,4,16,8,96]{5,3,2,4,1,0:T(8,128)(2,1)} %bitcast.346, ...), kind=kLoop, calls=%fused_computation.112 | loop fusion | flops 6291456 | bytes 6291472 | tf_op jit(solution)/shard_map/concatenate | solution.py:65
  30.5 4.0 copy.55
  44.0 4.4 copy.56
  48.4 5.0 %all-to-all-start = ((bf16[1,16,64,8,192]{4,3,1,0,2:T(8,128)(2,1)}), bf16[1,16,64,8,192]{4,3,1,0,2:T(8,128)(2,1)}, u32[]{:S(2)}, u32[]{:S(2)}) async-start(bf16[1,16,64,8,192]{4,3,1,0,2:T(8,128)(2,1)} %copy.56), calls=%async_computation | async-start | bytes 8388608 | tf_op jit(solution)/shard_map/all_to_all | solution.py:165
  61.7 12.7 %collective-permute-done.1 = bf16[1,16,16,8,192]{4,3,2,1,0:T(8,128)(2,1)} collective-permute-done((bf16[1,16,16,8,192]{4,3,2,1,0:T(8,128)(2,1)}, bf16[1,16,16,8,192]{4,3,2,1,0:T(8,128)(2,1)}, u32[]{:S(2)}, u32[]{:S(2)}) %collective-permute-start.1) | collective-permute-done | bytes 786464 | tf_op jit(solution)/shard_map/ppermute | solution.py:34
  74.4 3.9 maximum_bitcast_fusion
  78.3 5.1 %gather_fusion = bf16[4,16,16,8,192]{4,3,2,1,0:T(8,128)(2,1)} fusion(bf16[4,16,16,8,192]{4,3,2,1,0:T(8,128)(2,1)} %maximum_bitcast_fusion, s32[1024]{0:T(1024)} %pad_clamp_fusion), kind=kCustom, calls=%fused_computation | custom fusion | bytes 6291472 | tf_op jit(solution)/shard_map/gather | solution.py:35
  83.5 7.7 %fusion.61 = f32[1,64,16,8,192]{4,1,2,3,0:T(8,128)S(1)} fusion(bf16[64,16,8,192]{3,2,1,0:T(8,128)(2,1)} %bitcast.333), kind=kOutput, calls=%fused_computation.96 | convolution fusion | flops 201392128 | bytes 9437184 | tf_op jit(solution)/shard_map/kh,bhmnp->bkmnp/dot_general | solution.py:40
  91.2 4.9 %fusion.220 = (f32[1,64,16,8,96]{4,1,2,3,0:T(8,128)}, f32[1,64,16,8,96]{4,1,2,3,0:T(8,128)}) fusion(f32[1,64,16,8,192]{4,1,2,3,0:T(8,128)S(1)} %fusion.61), kind=kLoop, calls=%fused_computation.281 | loop fusion | flops 786432 | bytes 12582912 | tf_op jit(solution)/shard_map/slice | solution.py:59
  96.1 22.4 %all-to-all-done = bf16[1,16,64,8,192]{4,3,1,0,2:T(8,128)(2,1)} async-done(((bf16[1,16,64,8,192]{4,3,1,0,2:T(8,128)(2,1)}), bf16[1,16,64,8,192]{4,3,1,0,2:T(8,128)(2,1)}, u32[]{:S(2)}, u32[]{:S(2)}) %all-to-all-start) | async-done | bytes 3145760 | tf_op jit(solution)/shard_map/all_to_all | solution.py:165
  121.9 4.6 convolution_bitcast_fusion
  126.5 8.5 %fusion.222 = (f32[1,64,16,8,96]{4,1,3,2,0:T(8,128)S(1)}, f32[1,64,16,8,96]{4,1,3,2,0:T(8,128)}) fusion(f32[1,64,16,8,192]{4,1,3,2,0:T(8,128)} %convolution_bitcast_fusion), kind=kLoop, calls=%fused_computation.283 | loop fusion | flops 786432 | bytes 12582912 | tf_op jit(solution)/shard_map/slice | solution.py:59
  135.1 4.4 fusion.31
  154.1 4.8 %fusion.221 = (f32[1,64,16,8,96]{4,1,3,2,0:T(8,128)}, f32[1,64,16,8,96]{4,1,3,2,0:T(8,128)}) fusion(f32[1,64,16,8,192]{4,1,3,2,0:T(8,128)S(1)} %fusion.55), kind=kLoop, calls=%fused_computation.282 | loop fusion | flops 786432 | bytes 12582912 | tf_op jit(solution)/shard_map/slice | solution.py:59
  158.9 7.5 %fusion.9 = bf16[1,64,16,8,192]{4,1,3,2,0:T(8,128)(2,1)S(1)} fusion(f32[1,64,16,8,96]{4,1,3,2,0:T(8,128)} %get-tuple-element.39, f32[1,64,16,8,96]{4,1,3,2,0:T(8,128)} %get-tuple-element.38, f32[8,192,64,16]{1,2,3,0:T(8,128)} %copy-done.2, f32[8,192]{1,0:T(8,128)S(1)} %copy-done.20), kind=kOutput, calls=%fused_computation.18 | convolution fusion | flops 213975040 | bytes 15734784 | tf_op jit(solution)/shard_map/kh,bhmnp->bkmnp/dot_general | solution.py:40
  166.4 4.4 copy.61
  170.7 5.3 %all-to-all-start.1 = ((bf16[1,64,16,8,192]{4,3,2,0,1:T(8,128)(2,1)}), bf16[1,64,16,8,192]{4,3,2,0,1:T(8,128)(2,1)}, u32[]{:S(2)}, u32[]{:S(2)}) async-start(bf16[1,64,16,8,192]{4,3,2,0,1:T(8,128)(2,1)} %copy.61), calls=%async_computation.1 | async-start | bytes 8388608 | tf_op jit(solution)/shard_map/all_to_all | solution.py:171
  176.0 16.3 %convert_reduce_fusion.1 = (f32[8,192]{1,0:T(8,128)}, bf16[1,64,16,8,192]{4,1,2,3,0:T(8,128)(2,1)S(1)}) fusion(f32[8,192]{1,0:T(8,128)} %param.14, f32[8,192,64,16]{1,2,3,0:T(8,128)} %copy-done.2, f32[1,64,16,8,96]{4,1,2,3,0:T(8,128)} %get-tuple-element.37, f32[1,64,16,8,96]{4,1,2,3,0:T(8,128)} %get-tuple-element.36, bf16[64,16,8,192]{3,2,1,0:T(8,128)(2,1)} %bitcast.334), kind=kOutput, calls=%fused_computation.30 | convolution fusion | flops 218692096 | bytes 18886656 | tf_op jit(solution)/shard_map/kh,bhmnp->bkmnp/dot_general | solution.py:40
  192.4 11.1 %convert_reduce_fusion.2 = (f32[8,192]{1,0:T(8,128)}, bf16[1,64,16,8,192]{4,1,2,3,0:T(8,128)(2,1)S(1)}) fusion(f32[8,192]{1,0:T(8,128)S(1)} %copy-done.28, f32[8,192,64,16]{1,2,3,0:T(8,128)} %copy-done.6, bf16[1,64,16,8,192]{4,1,2,3,0:T(8,128)(2,1)S(1)} %get-tuple-element.59, bf16[8,96,96]{2,1,0:T(8,128)(2,1)S(1)} %copy-done.17, ...), kind=kOutput, calls=%fused_computation.31 | convolution fusion | flops 640940544 | bytes 13037568 | tf_op jit(solution)/shard_map/bkmnq,npq->bkmnp/dot_general | solution.py:40
  205.5 4.6 fusion.58
  210.1 8.5 %fusion.219 = (f32[1,64,16,8,96]{4,1,3,2,0:T(8,128)S(1)}, f32[1,64,16,8,96]{4,1,3,2,0:T(8,128)}) fusion(f32[1,64,16,8,192]{4,1,3,2,0:T(8,128)} %fusion.58), kind=kLoop, calls=%fused_computation.280 | loop fusion | flops 786432 | bytes 12582912 | tf_op jit(solution)/shard_map/slice | solution.py:59
  218.6 4.2 fusion.11
  222.8 4.4 copy.75
  232.0 4.4 fusion.78
  236.4 4.9 %all-to-all-start.2 = ((bf16[1,64,16,8,192]{4,3,2,0,1:T(8,128)(2,1)}), bf16[1,64,16,8,192]{4,3,2,0,1:T(8,128)(2,1)}, u32[]{:S(2)}, u32[]{:S(2)}) async-start(bf16[1,64,16,8,192]{4,3,2,0,1:T(8,128)(2,1)} %copy.75), calls=%async_computation.2 | async-start | bytes 8388608 | tf_op jit(solution)/shard_map/all_to_all | solution.py:182
  246.3 137.3 %all-reduce.4.cloned.1.call-done = (f32[2,8,96,96]{3,2,1,0:T(8,128)}, f32[2,8,96,96]{3,2,1,0:T(8,128)}) async-done(((f32[2,8,96,96]{3,2,1,0:T(8,128)}, f32[2,8,96,96]{3,2,1,0:T(8,128)}), (f32[2,8,96,96]{3,2,1,0:T(8,128)}, f32[2,8,96,96]{3,2,1,0:T(8,128)})) %all-reduce.4.cloned.1.call-update) | async-done | bytes 1179664 | tf_op jit(solution)/shard_map/psum | solution.py:199
  391.2 5.6 %convolution_subtract_fusion.1 = f32[128,16,8,96]{0,3,2,1:T(8,128)} fusion(f32[128,16,8,96]{0,3,2,1:T(8,128)S(1)} %fusion.73, bf16[1,16,64,8,192]{4,2,3,1,0:T(8,128)(2,1)S(1)} %bitcast.344, f32[64]{0:T(128)S(1)} %copy-done.26), kind=kOutput, calls=%fused_computation.99 | convolution fusion | flops 203030528 | bytes 14680576 | tf_op jit(solution)/shard_map/bhmnp,mw->bhwnp/dot_general | solution.py:40
  404.2 4.5 fusion.25
  408.8 6.1 %fusion.27 = (bf16[1,16,128,768]{2,3,1,0:T(8,128)(2,1)}, bf16[1,16,128,768]{2,3,1,0:T(8,128)(2,1)}) fusion(bf16[1,16,128,768]{2,3,1,0:T(8,128)(2,1)S(1)} %copy.55, bf16[1,16,128,768]{2,3,1,0:T(8,128)(2,1)S(1)} %copy-done.1, f32[16,128]{1,0:T(8,128)S(1)} %get-tuple-element.60, f32[16,128]{1,0:T(8,128)S(1)} %get-tuple-element.61, f32[768]{0:T(1024)S(1)} %copy-done.19, ...), kind=kLoop, calls=%fused_computation.48 | loop fusion | flops 29884416 | bytes 25204736 | tf_op jit(solution)/shard_map/convert_element_type | solution.py:188
  414.8 4.8 %copy.79 = bf16[1,16,128,768]{3,2,1,0:T(8,128)(2,1)} copy(bf16[1,16,128,768]{2,3,1,0:T(8,128)(2,1)} %get-tuple-element.46) | data formatting | bytes 6291456
  422.4 39.4 %all-reduce = (f32[8,192]{1,0:T(8,128)S(1)}, f32[8,192]{1,0:T(8,128)S(1)}, f32[768]{0:T(1024)S(1)}, f32[768]{0:T(1024)S(1)}) all-reduce(f32[8,192]{1,0:T(8,128)S(1)} %copy-done.24, f32[8,192]{1,0:T(8,128)S(1)} %copy-done.21, f32[768]{0:T(1024)S(1)} %get-tuple-element.24, ...), channel_id=1, replica_groups=mesh['dp'=8,'spatial'=4] {'dp','spatial'}, use_global_device_ids=true, to_apply=%region_6.7 | all-reduce | flops 4608 | bytes 36864 | tf_op jit(solution)/shard_map/psum | solution.py:199
  (118 shorter events, 80.8 us)
Async XLA Ops:
  7.2 7.3 %copy-start.25 = (f32[64]{0:T(128)}, f32[64]{0:T(128)S(1)}, u32[]{:S(2)}) copy-start(f32[64]{0:T(128)S(1)} %fusion.142) | copy-start | bytes 772
  10.7 7.5 %copy-start = (bf16[1,16,128,768]{2,3,1,0:T(8,128)(2,1)}, bf16[1,16,128,768]{2,3,1,0:T(8,128)(2,1)S(1)}, u32[]{:S(2)}) copy-start(bf16[1,16,128,768]{2,3,1,0:T(8,128)(2,1)S(1)} %copy.63) | copy-start | bytes 9437188
  24.6 37.1 %collective-permute-start.2 = (bf16[1,16,16,8,192]{4,3,2,1,0:T(8,128)(2,1)}, bf16[1,16,16,8,192]{4,3,2,1,0:T(8,128)(2,1)}, u32[]{:S(2)}, u32[]{:S(2)}) collective-permute-start(bf16[1,16,16,8,192]{4,3,2,1,0:T(8,128)(2,1)} %bitcast.327), channel_id=1, source_target_pairs={{0,3},{1,2},{2,1},{3,0},{4,7},{5,6},{6,5},{7,4},{8,11},{9,10},{10,... | collective-permute-start | bytes 2359304 | tf_op jit(solution)/shard_map/ppermute | solution.py:34
  28.5 45.9 %collective-permute-start.1 = (bf16[1,16,16,8,192]{4,3,2,1,0:T(8,128)(2,1)}, bf16[1,16,16,8,192]{4,3,2,1,0:T(8,128)(2,1)}, u32[]{:S(2)}, u32[]{:S(2)}) collective-permute-start(bf16[1,16,16,8,192]{4,3,2,1,0:T(8,128)(2,1)} %bitcast.328), channel_id=1, source_target_pairs={{0,2},{1,3},{2,0},{3,1},{4,6},{5,7},{6,4},{7,5},{8,10},{9,11},{10,... | collective-permute-start | bytes 2359304 | tf_op jit(solution)/shard_map/ppermute | solution.py:34
  30.4 44.0 %collective-permute-start = (bf16[1,16,16,8,192]{4,3,2,1,0:T(8,128)(2,1)}, bf16[1,16,16,8,192]{4,3,2,1,0:T(8,128)(2,1)}, u32[]{:S(2)}, u32[]{:S(2)}) collective-permute-start(bf16[1,16,16,8,192]{4,3,2,1,0:T(8,128)(2,1)} %bitcast.329), channel_id=1, source_target_pairs={{0,1},{1,0},{2,3},{3,2},{4,5},{5,4},{6,7},{7,6},{8,9},{9,8},{10,11... | collective-permute-start | bytes 2359304 | tf_op jit(solution)/shard_map/ppermute | solution.py:34
  48.4 70.1 %all-to-all-start = ((bf16[1,16,64,8,192]{4,3,1,0,2:T(8,128)(2,1)}), bf16[1,16,64,8,192]{4,3,1,0,2:T(8,128)(2,1)}, u32[]{:S(2)}, u32[]{:S(2)}) async-start(bf16[1,16,64,8,192]{4,3,1,0,2:T(8,128)(2,1)} %copy.56), calls=%async_computation | async-start | bytes 8388608 | tf_op jit(solution)/shard_map/all_to_all | solution.py:165
  135.1 4.4 copy-start.10
  139.5 5.3 %copy-start.12 = (bf16[8,96,96]{2,1,0:T(8,128)(2,1)S(1)}, bf16[8,96,96]{2,1,0:T(8,128)(2,1)}, u32[]{:S(2)}) copy-start(bf16[8,96,96]{2,1,0:T(8,128)(2,1)} %fusion.217) | copy-start | bytes 442372
  139.5 5.3 %copy-start.14 = (bf16[8,96,96]{2,1,0:T(8,128)(2,1)S(1)}, bf16[8,96,96]{2,1,0:T(8,128)(2,1)}, u32[]{:S(2)}) copy-start(bf16[8,96,96]{2,1,0:T(8,128)(2,1)} %get-tuple-element.52) | copy-start | bytes 442372
  139.5 5.3 %copy-start.16 = (bf16[8,96,96]{2,1,0:T(8,128)(2,1)S(1)}, bf16[8,96,96]{2,1,0:T(8,128)(2,1)}, u32[]{:S(2)}) copy-start(bf16[8,96,96]{2,1,0:T(8,128)(2,1)} %get-tuple-element.53) | copy-start | bytes 442372
  139.5 5.3 %copy-start.27 = (f32[8,192]{1,0:T(8,128)S(1)}, f32[8,192]{1,0:T(8,128)}, u32[]{:S(2)}) copy-start(f32[8,192]{1,0:T(8,128)} %param.12) | copy-start | bytes 18436
  141.5 3.3 copy-start.6
  144.8 7.0 %copy-start.20 = (f32[8,192]{1,0:T(8,128)S(1)}, f32[8,192]{1,0:T(8,128)}, u32[]{:S(2)}) copy-start(f32[8,192]{1,0:T(8,128)} %param.14) | copy-start | bytes 18436
  148.5 3.2 copy-start.2
  170.7 65.6 %all-to-all-start.1 = ((bf16[1,64,16,8,192]{4,3,2,0,1:T(8,128)(2,1)}), bf16[1,64,16,8,192]{4,3,2,0,1:T(8,128)(2,1)}, u32[]{:S(2)}, u32[]{:S(2)}) async-start(bf16[1,64,16,8,192]{4,3,2,0,1:T(8,128)(2,1)} %copy.61), calls=%async_computation.1 | async-start | bytes 8388608 | tf_op jit(solution)/shard_map/all_to_all | solution.py:171
  176.0 16.3 %copy-start.13 = (bf16[8,96,96]{2,1,0:T(8,128)(2,1)S(1)}, bf16[8,96,96]{2,1,0:T(8,128)(2,1)}, u32[]{:S(2)}) copy-start(bf16[8,96,96]{2,1,0:T(8,128)(2,1)} %fusion.217) | copy-start | bytes 442372
  176.0 16.3 %copy-start.15 = (bf16[8,96,96]{2,1,0:T(8,128)(2,1)S(1)}, bf16[8,96,96]{2,1,0:T(8,128)(2,1)}, u32[]{:S(2)}) copy-start(bf16[8,96,96]{2,1,0:T(8,128)(2,1)} %get-tuple-element.52) | copy-start | bytes 442372
  176.0 16.3 %copy-start.17 = (bf16[8,96,96]{2,1,0:T(8,128)(2,1)S(1)}, bf16[8,96,96]{2,1,0:T(8,128)(2,1)}, u32[]{:S(2)}) copy-start(bf16[8,96,96]{2,1,0:T(8,128)(2,1)} %get-tuple-element.53) | copy-start | bytes 442372
  176.0 16.3 %copy-start.28 = (f32[8,192]{1,0:T(8,128)S(1)}, f32[8,192]{1,0:T(8,128)}, u32[]{:S(2)}) copy-start(f32[8,192]{1,0:T(8,128)} %param.12) | copy-start | bytes 18436
  192.3 11.2 %copy-start.8 = (bf16[1,64,16,8,192]{4,1,2,3,0:T(8,128)(2,1)}, bf16[1,64,16,8,192]{4,1,2,3,0:T(8,128)(2,1)S(1)}, u32[]{:S(2)}) copy-start(bf16[1,64,16,8,192]{4,1,2,3,0:T(8,128)(2,1)S(1)} %get-tuple-element.59) | copy-start | bytes 9437188
  192.4 11.2 %copy-start.11 = (bf16[8,96,96]{2,1,0:T(8,128)(2,1)S(1)}, bf16[8,96,96]{2,1,0:T(8,128)(2,1)}, u32[]{:S(2)}) copy-start(bf16[8,96,96]{2,1,0:T(8,128)(2,1)} %get-tuple-element.55) | copy-start | bytes 442372
  222.8 4.5 copy-start.4
  222.8 9.2 %slice-start.2 = ((s8[8388608]{0:T(1024)(128)(4,1)}), s8[4194304]{0:T(1024)(128)(4,1)S(1)}, s32[]{:S(2)}) async-start(s8[8388608]{0:T(1024)(128)(4,1)} %bitcast.347), calls=%async_computation.6 | async-start | bytes 8388608
  227.3 4.7 %slice-start.3 = ((s8[8388608]{0:T(1024)(128)(4,1)}), s8[4194304]{0:T(1024)(128)(4,1)S(1)}, s32[]{:S(2)}) async-start(s8[8388608]{0:T(1024)(128)(4,1)} %bitcast.347), calls=%async_computation.7 | async-start | bytes 8388608
  227.3 4.7 %copy-start.9 = (bf16[1,64,16,8,192]{4,1,2,3,0:T(8,128)(2,1)S(1)}, bf16[1,64,16,8,192]{4,1,2,3,0:T(8,128)(2,1)}, u32[]{:S(2)}) copy-start(bf16[1,64,16,8,192]{4,1,2,3,0:T(8,128)(2,1)} %copy-done.8) | copy-start | bytes 9437188
  236.4 160.4 %all-to-all-start.2 = ((bf16[1,64,16,8,192]{4,3,2,0,1:T(8,128)(2,1)}), bf16[1,64,16,8,192]{4,3,2,0,1:T(8,128)(2,1)}, u32[]{:S(2)}, u32[]{:S(2)}) async-start(bf16[1,64,16,8,192]{4,3,2,0,1:T(8,128)(2,1)} %copy.75), calls=%async_computation.2 | async-start | bytes 8388608 | tf_op jit(solution)/shard_map/all_to_all | solution.py:182
  241.3 142.4 %all-reduce.4.cloned.1.call-start = ((), (), s32[]{:S(2)}) async-start(), calls=%async_computation.3 | async-start | bytes 3145728 | tf_op jit(solution)/shard_map/psum | solution.py:199
  386.3 3.4 copy-start.26
  400.2 8.5 %slice-start = ((s8[6291456]{0:T(1024)(128)(4,1)}), s8[4194304]{0:T(1024)(128)(4,1)S(1)}, s32[]{:S(2)}) async-start(s8[6291456]{0:T(1024)(128)(4,1)} %bitcast.339), calls=%async_computation.4 | async-start | bytes 8388608
  401.6 7.1 %slice-start.1 = ((s8[6291456]{0:T(1024)(128)(4,1)}), s8[2097152]{0:T(1024)(128)(4,1)S(1)}, s32[]{:S(2)}) async-start(s8[6291456]{0:T(1024)(128)(4,1)} %bitcast.339), calls=%async_computation.5 | async-start | bytes 4194304
  404.2 4.5 copy-start.23
  414.8 4.8 %copy-start.5 = (bf16[1,16,128,768]{2,3,1,0:T(8,128)(2,1)S(1)}, bf16[1,16,128,768]{2,3,1,0:T(8,128)(2,1)}, u32[]{:S(2)}) copy-start(bf16[1,16,128,768]{2,3,1,0:T(8,128)(2,1)} %get-tuple-element.47) | copy-start | bytes 9437188
  (8 other events, 17.4 us)
Sparse Core Ops, SparseCore 0:
  248.1 135.5 all-reduce.3
